TPU v7x, 32 devices: a whole 2x2x4 slice. The times are simulated.
32 devices in a mesh: groups: 2 (over y), freq: 4 (over x, core), recv: 4 (over z).
Axes of the slice: x: 2, y: 2, z: 4, core: 2. Of those that a mesh axis runs over, the one named last changes fastest.
Arguments:
- operator: bfloat16 [4, 32, 512, 2048], P('groups', 'freq', 'recv'), parts along dimension 0, may hold values from -0.125 to 0.125
- recorded: float32 [4, 32, 8, 512], P('groups', 'freq', None, 'recv'), parts along dimension 0, may hold values from -18 to 18
- win_start: int32 [16, 16], P('groups'), parts along dimension 0, may hold values from 0 to 15
- win_end: int32 [16, 16], P('groups'), parts along dimension 0, may hold values from 17 to 32
Outputs:
- reflectivity: float32 [4, 32, 8, 2048], P('groups', 'freq', None, 'recv'), parts along dimension 0
- residual: float32 [4, 32, 8, 512], P('groups', 'freq', None, 'recv'), parts along dimension 0
There are 2 independent parts, one for each index of `groups`. A program takes and returns all parts, laid end to end along the dimension named above; each array names one. Nothing has to cross between parts.
All inputs are finite; a program needn't handle non-finite values.
Results may differ from a plain program's by a relative error of at most 0.013.
Values may be sent and summed in bfloat16 or wider, within the bound.
No kernel may reach another device: no remote copies, remote signals or barrier semaphores. Data moves between devices by JAX's collectives and lax.ppermute only.
A program may use at most 64 MiB of HBM per device.

v0:
```python
import math
import jax
import jax.numpy as jnp
from jax import lax
from jax.sharding import PartitionSpec as P

SBLK = 128
ITERS = 5


def high_dot(left, right):
    return jnp.dot(left, right, precision=lax.Precision.HIGHEST)


def dft_rows(row_ids, length):
    positions = jnp.arange(length, dtype=jnp.int32)
    phases = (row_ids[:, None] * positions[None, :] % length).astype(jnp.float32) * (
        2.0 * math.pi / length
    )
    normalizer = 1.0 / math.sqrt(length)
    return (jnp.cos(phases) * normalizer, jnp.sin(phases) * normalizer)


def to_time(real_part, imag_part, cos_rows, sin_rows):
    time_real = high_dot(cos_rows.T, real_part) - high_dot(sin_rows.T, imag_part)
    time_imag = high_dot(sin_rows.T, real_part) + high_dot(cos_rows.T, imag_part)
    return (time_real, time_imag)


def to_freq(kept_real, kept_imag, cos_rows, sin_rows):
    real_part = high_dot(cos_rows, kept_real) + high_dot(sin_rows, kept_imag)
    imag_part = high_dot(cos_rows, kept_imag) - high_dot(sin_rows, kept_real)
    return jnp.stack([real_part, imag_part])


def window_mask(column_ids, src_local, win_start, win_end, length):
    blocks = win_start.shape[1]
    side_ids = column_ids // src_local
    source_ids = lax.axis_index("recv") * src_local + column_ids % src_local
    flat_ids = side_ids * blocks + source_ids // SBLK
    table_ids = jnp.arange(win_start.shape[0] * blocks, dtype=jnp.int32)
    matches = flat_ids[:, None] == table_ids[None, :]
    opening = jnp.sum(jnp.where(matches, win_start.reshape(-1)[None, :], 0), axis=1)
    closing = jnp.sum(jnp.where(matches, win_end.reshape(-1)[None, :], 0), axis=1)
    samples = jnp.arange(length, dtype=jnp.int32)[:, None]
    return ((samples >= opening[None, :]) & (samples < closing[None, :])).astype(jnp.float32)


def on_device(operator, recorded, win_start, win_end):
    freq_local = operator.shape[1]
    sources = operator.shape[3]
    right_sides = recorded.shape[2]
    src_local = sources // lax.axis_size("recv")
    total_freq = freq_local * lax.axis_size("freq")
    columns = right_sides * src_local
    real_operator = operator[0]
    imag_operator = operator[1]
    reflect = jnp.zeros((2, freq_local, right_sides, src_local), jnp.float32)
    residual = recorded
    for iteration in range(ITERS):
        rounded_residual = residual.astype(jnp.bfloat16)
        partial_real = jnp.einsum(
            "fbr,frs->fbs", rounded_residual[0], real_operator, preferred_element_type=jnp.float32
        ) + jnp.einsum(
            "fbr,frs->fbs", rounded_residual[1], imag_operator, preferred_element_type=jnp.float32
        )
        partial_imag = jnp.einsum(
            "fbr,frs->fbs", rounded_residual[1], real_operator, preferred_element_type=jnp.float32
        ) - jnp.einsum(
            "fbr,frs->fbs", rounded_residual[0], imag_operator, preferred_element_type=jnp.float32
        )
        gradient = lax.psum_scatter(
            jnp.stack([partial_real, partial_imag]).astype(jnp.bfloat16),
            "recv",
            scatter_dimension=3,
            tiled=True,
        ).astype(jnp.float32)
        flattened = gradient.reshape(2, freq_local, columns)
        empty_time = jnp.zeros((2, total_freq, columns), jnp.float32)
        segment = lax.all_gather(flattened.astype(jnp.bfloat16), "freq", axis=1, tiled=True).astype(
            jnp.float32
        )
        row_ids = jnp.arange(segment.shape[1], dtype=jnp.int32)
        cos_part, sin_part = dft_rows(row_ids, total_freq)
        part_real, part_imag = to_time(segment[0], segment[1], cos_part, sin_part)
        timed = empty_time + jnp.stack([part_real, part_imag])
        window = window_mask(
            jnp.arange(columns, dtype=jnp.int32), src_local, win_start, win_end, total_freq
        )
        own_rows = lax.axis_index("freq") * freq_local + jnp.arange(freq_local, dtype=jnp.int32)
        cos_rows, sin_rows = dft_rows(own_rows, total_freq)
        projected = to_freq(timed[0] * window, timed[1] * window, cos_rows, sin_rows)
        direction = projected.reshape(2, freq_local, right_sides, src_local)
        rounded_direction = direction.astype(jnp.bfloat16)
        add_segment = lax.all_gather(rounded_direction, "recv", axis=3, tiled=True)
        image_real = jnp.einsum(
            "fbs,frs->fbr", add_segment[0], real_operator, preferred_element_type=jnp.float32
        ) - jnp.einsum(
            "fbs,frs->fbr", add_segment[1], imag_operator, preferred_element_type=jnp.float32
        )
        image_imag = jnp.einsum(
            "fbs,frs->fbr", add_segment[0], imag_operator, preferred_element_type=jnp.float32
        ) + jnp.einsum(
            "fbs,frs->fbr", add_segment[1], real_operator, preferred_element_type=jnp.float32
        )
        image = jnp.stack([image_real, image_imag])
        direction_power, image_energy = lax.psum(
            (jnp.sum(direction * direction), jnp.sum(image * image)), ("freq", "recv")
        )
        step_length = direction_power / (image_energy + 1e-06)
        reflect = reflect + step_length * direction
        residual = residual - step_length * image
    return (reflect, residual)


def solution(mesh):
    return jax.shard_map(
        on_device,
        mesh=mesh,
        in_specs=(
            P("groups", "freq", "recv", None),
            P("groups", "freq", None, "recv"),
            P("groups", None),
            P("groups", None),
        ),
        out_specs=(P("groups", "freq", None, "recv"), P("groups", "freq", None, "recv")),
        check_vma=False,
    )
```

profile of v0, /device:TPU:0, one launch (start us, length us, event | category | flops | bytes accessed | tf_op | source)
XLA Modules:
  0.0 536.4 jit_solution(5900010467713200672)
XLA Ops:
  8.1 3.0 fusion.46
  11.0 3.3 fusion.48
  16.9 1.8 select_reduce_fusion.1
  18.7 22.4 %reduce-scatter.6.cloned.1.call-done = bf16[2,8,8,512]{3,2,1,0:T(8,128)(2,1)} async-done(((bf16[2,8,8,2048]{3,2,1,0:T(8,128)(2,1)}), bf16[2,8,8,512]{3,2,1,0:T(8,128)(2,1)}) %reduce-scatter.6.cloned.1.call-update) | async-done | bytes 131088 | tf_op jit(solution)/shard_map/reduce_scatter | solution.py:72
  41.1 1.0 convert_element_type.125
  42.1 7.1 %all_gather.30 = bf16[2,32,4096]{2,1,0:T(8,128)(2,1)S(1)} all-gather(bf16[2,8,4096]{2,1,0:T(8,128)(2,1)S(1)} %convert_element_type.125), channel_id=1, replica_groups=mesh['groups'=2,'freq'=4,'recv'=4] {'freq'}, dimensions={1}, use_global_device_ids=true | all-gather | bytes 655360 | tf_op jit(solution)/shard_map/all_gather | solution.py:80
  54.0 16.1 %all_gather.31 = bf16[2,8,8,2048]{3,2,1,0:T(8,128)(2,1)S(1)} all-gather(bf16[2,8,8,512]{3,2,1,0:T(8,128)(2,1)S(1)} %get-tuple-element.27), channel_id=1, replica_groups=mesh['groups'=2,'freq'=4,'recv'=4] {'recv'}, dimensions={3}, use_global_device_ids=true | all-gather | bytes 655360 | tf_op jit(solution)/shard_map/all_gather | solution.py:95
  70.1 3.5 fusion.42
  73.6 3.4 fusion.44
  77.1 1.2 fusion.189
  78.2 1.2 fusion.183
  80.1 30.5 %all-reduce.4 = (f32[]{:T(128)}, f32[]{:T(128)}) all-reduce(f32[]{:T(128)} %get-tuple-element.26, f32[]{:T(128)} %multiply_reduce_fusion.9), channel_id=1, replica_groups=mesh['groups'=2,'freq'=4,'recv'=4] {'freq','recv'}, use_global_device_ids=true, to_apply=%region_4.5 | all-reduce | flops 2 | bytes 16 | tf_op jit(solution)/shard_map/psum | solution.py:107
  111.9 2.8 fusion.38
  114.7 2.8 fusion.40
  117.6 2.9 fusion.159
  120.4 2.9 fusion.156
  124.2 21.0 %reduce-scatter.8.cloned.1.call-done = bf16[2,8,8,512]{3,2,1,0:T(8,128)(2,1)} async-done(((bf16[2,8,8,2048]{3,2,1,0:T(8,128)(2,1)}), bf16[2,8,8,512]{3,2,1,0:T(8,128)(2,1)}) %reduce-scatter.8.cloned.1.call-update) | async-done | bytes 131088 | tf_op jit(solution)/shard_map/reduce_scatter | solution.py:72
  145.2 1.0 convert_element_type.128
  146.2 7.1 %all_gather.32 = bf16[2,32,4096]{2,1,0:T(8,128)(2,1)S(1)} all-gather(bf16[2,8,4096]{2,1,0:T(8,128)(2,1)S(1)} %convert_element_type.128), channel_id=1, replica_groups=mesh['groups'=2,'freq'=4,'recv'=4] {'freq'}, dimensions={1}, use_global_device_ids=true | all-gather | bytes 655360 | tf_op jit(solution)/shard_map/all_gather | solution.py:80
  158.2 16.1 %all_gather.33 = bf16[2,8,8,2048]{3,2,1,0:T(8,128)(2,1)S(1)} all-gather(bf16[2,8,8,512]{3,2,1,0:T(8,128)(2,1)S(1)} %get-tuple-element.25), channel_id=1, replica_groups=mesh['groups'=2,'freq'=4,'recv'=4] {'recv'}, dimensions={3}, use_global_device_ids=true | all-gather | bytes 655360 | tf_op jit(solution)/shard_map/all_gather | solution.py:95
  174.2 3.5 fusion.34
  177.8 3.4 fusion.36
  181.1 1.2 fusion.201
  182.3 1.2 fusion.195
  184.2 30.5 %all-reduce.3 = (f32[]{:T(128)}, f32[]{:T(128)}) all-reduce(f32[]{:T(128)} %get-tuple-element.24, f32[]{:T(128)} %multiply_reduce_fusion.8), channel_id=1, replica_groups=mesh['groups'=2,'freq'=4,'recv'=4] {'freq','recv'}, use_global_device_ids=true, to_apply=%region_9.10 | all-reduce | flops 2 | bytes 16 | tf_op jit(solution)/shard_map/psum | solution.py:107
  216.0 2.8 fusion.30
  218.9 2.8 fusion.32
  221.7 2.9 fusion.165
  224.6 2.9 fusion.162
  228.4 21.0 %reduce-scatter.10.cloned.1.call-done = bf16[2,8,8,512]{3,2,1,0:T(8,128)(2,1)} async-done(((bf16[2,8,8,2048]{3,2,1,0:T(8,128)(2,1)}), bf16[2,8,8,512]{3,2,1,0:T(8,128)(2,1)}) %reduce-scatter.10.cloned.1.call-update) | async-done | bytes 131088 | tf_op jit(solution)/shard_map/reduce_scatter | solution.py:72
  249.3 1.0 convert_element_type.131
  250.3 7.1 %all_gather.34 = bf16[2,32,4096]{2,1,0:T(8,128)(2,1)S(1)} all-gather(bf16[2,8,4096]{2,1,0:T(8,128)(2,1)S(1)} %convert_element_type.131), channel_id=1, replica_groups=mesh['groups'=2,'freq'=4,'recv'=4] {'freq'}, dimensions={1}, use_global_device_ids=true | all-gather | bytes 655360 | tf_op jit(solution)/shard_map/all_gather | solution.py:80
  262.3 16.1 %all_gather.35 = bf16[2,8,8,2048]{3,2,1,0:T(8,128)(2,1)S(1)} all-gather(bf16[2,8,8,512]{3,2,1,0:T(8,128)(2,1)S(1)} %get-tuple-element.23), channel_id=1, replica_groups=mesh['groups'=2,'freq'=4,'recv'=4] {'recv'}, dimensions={3}, use_global_device_ids=true | all-gather | bytes 655360 | tf_op jit(solution)/shard_map/all_gather | solution.py:95
  278.4 3.5 fusion.26
  281.9 3.4 fusion.28
  285.3 1.2 fusion.213
  286.5 1.2 fusion.207
  288.3 30.7 %all-reduce.2 = (f32[]{:T(128)}, f32[]{:T(128)}) all-reduce(f32[]{:T(128)} %get-tuple-element.22, f32[]{:T(128)} %multiply_reduce_fusion.7), channel_id=1, replica_groups=mesh['groups'=2,'freq'=4,'recv'=4] {'freq','recv'}, use_global_device_ids=true, to_apply=%region_14.15 | all-reduce | flops 2 | bytes 16 | tf_op jit(solution)/shard_map/psum | solution.py:107
  320.3 2.8 fusion.22
  323.2 2.8 fusion.24
  326.0 2.9 fusion.171
  328.9 2.9 fusion.168
  332.7 20.9 %reduce-scatter.12.cloned.1.call-done = bf16[2,8,8,512]{3,2,1,0:T(8,128)(2,1)} async-done(((bf16[2,8,8,2048]{3,2,1,0:T(8,128)(2,1)}), bf16[2,8,8,512]{3,2,1,0:T(8,128)(2,1)}) %reduce-scatter.12.cloned.1.call-update) | async-done | bytes 131088 | tf_op jit(solution)/shard_map/reduce_scatter | solution.py:72
  353.6 1.0 convert_element_type.134
  354.5 7.2 %all_gather.36 = bf16[2,32,4096]{2,1,0:T(8,128)(2,1)S(1)} all-gather(bf16[2,8,4096]{2,1,0:T(8,128)(2,1)S(1)} %convert_element_type.134), channel_id=1, replica_groups=mesh['groups'=2,'freq'=4,'recv'=4] {'freq'}, dimensions={1}, use_global_device_ids=true | all-gather | bytes 655360 | tf_op jit(solution)/shard_map/all_gather | solution.py:80
  366.6 16.1 %all_gather.37 = bf16[2,8,8,2048]{3,2,1,0:T(8,128)(2,1)S(1)} all-gather(bf16[2,8,8,512]{3,2,1,0:T(8,128)(2,1)S(1)} %get-tuple-element.21), channel_id=1, replica_groups=mesh['groups'=2,'freq'=4,'recv'=4] {'recv'}, dimensions={3}, use_global_device_ids=true | all-gather | bytes 655360 | tf_op jit(solution)/shard_map/all_gather | solution.py:95
  382.7 3.5 fusion.18
  386.2 3.4 fusion.20
  389.6 1.2 fusion.225
  390.8 1.2 fusion.219
  392.6 30.5 %all-reduce.1 = (f32[]{:T(128)}, f32[]{:T(128)}) all-reduce(f32[]{:T(128)} %get-tuple-element.20, f32[]{:T(128)} %multiply_reduce_fusion.6), channel_id=1, replica_groups=mesh['groups'=2,'freq'=4,'recv'=4] {'freq','recv'}, use_global_device_ids=true, to_apply=%region_19.20 | all-reduce | flops 2 | bytes 16 | tf_op jit(solution)/shard_map/psum | solution.py:107
  424.4 2.8 fusion.14
  427.3 2.8 fusion.16
  430.1 2.9 fusion.177
  433.0 2.9 fusion.174
  436.7 20.9 %reduce-scatter.14.cloned.1.call-done = bf16[2,8,8,512]{3,2,1,0:T(8,128)(2,1)} async-done(((bf16[2,8,8,2048]{3,2,1,0:T(8,128)(2,1)}), bf16[2,8,8,512]{3,2,1,0:T(8,128)(2,1)}) %reduce-scatter.14.cloned.1.call-update) | async-done | bytes 131088 | tf_op jit(solution)/shard_map/reduce_scatter | solution.py:72
  457.6 1.0 convert_element_type.137
  458.6 7.1 %all_gather.38 = bf16[2,32,4096]{2,1,0:T(8,128)(2,1)S(1)} all-gather(bf16[2,8,4096]{2,1,0:T(8,128)(2,1)S(1)} %convert_element_type.137), channel_id=1, replica_groups=mesh['groups'=2,'freq'=4,'recv'=4] {'freq'}, dimensions={1}, use_global_device_ids=true | all-gather | bytes 655360 | tf_op jit(solution)/shard_map/all_gather | solution.py:80
  470.5 16.1 %all_gather.39 = bf16[2,8,8,2048]{3,2,1,0:T(8,128)(2,1)S(1)} all-gather(bf16[2,8,8,512]{3,2,1,0:T(8,128)(2,1)S(1)} %get-tuple-element.18), channel_id=1, replica_groups=mesh['groups'=2,'freq'=4,'recv'=4] {'recv'}, dimensions={3}, use_global_device_ids=true | all-gather | bytes 655360 | tf_op jit(solution)/shard_map/all_gather | solution.py:95
  486.6 3.5 fusion.10
  490.2 3.4 fusion.12
  493.6 1.2 fusion.237
  494.8 1.2 fusion.231
  496.6 30.3 %all-reduce = (f32[]{:T(128)}, f32[]{:T(128)}) all-reduce(f32[]{:T(128)} %get-tuple-element.19, f32[]{:T(128)} %multiply_reduce_fusion.5), channel_id=1, replica_groups=mesh['groups'=2,'freq'=4,'recv'=4] {'freq','recv'}, use_global_device_ids=true, to_apply=%region_24.25 | all-reduce | flops 2 | bytes 16 | tf_op jit(solution)/shard_map/psum | solution.py:107
  (121 shorter events, 35.6 us)
Async XLA Ops:
  7.2 34.0 %reduce-scatter.6.cloned.1.call-start = ((), (), s32[]{:S(2)}) async-start(), calls=%async_computation.5 | async-start | bytes 655360 | tf_op jit(solution)/shard_map/reduce_scatter | solution.py:72
  8.1 6.3 %copy-start = (bf16[2,8,128,2048]{3,2,1,0:T(8,128)(2,1)S(1)}, bf16[2,8,128,2048]{3,2,1,0:T(8,128)(2,1)}, u32[]{:S(2)}) copy-start(bf16[2,8,128,2048]{3,2,1,0:T(8,128)(2,1)} %param.4) | copy-start | bytes 25165828
  15.1 1.6 copy-start.2
  15.1 1.7 copy-start.3
  16.6 128.6 %reduce-scatter.8.cloned.1.call-start = ((), (), s32[]{:S(2)}) async-start(), calls=%async_computation.6 | async-start | bytes 655360 | tf_op jit(solution)/shard_map/reduce_scatter | solution.py:72
  50.2 26.9 %slice-start = ((s8[8388608]{0:T(1024)(128)(4,1)}), s8[4194304]{0:T(1024)(128)(4,1)S(1)}, s32[]{:S(2)}) async-start(s8[8388608]{0:T(1024)(128)(4,1)} %bitcast.406), calls=%async_computation.10 | async-start | bytes 8388608
  70.1 6.9 %slice-start.1 = ((s8[8388608]{0:T(1024)(128)(4,1)}), s8[4194304]{0:T(1024)(128)(4,1)S(1)}, s32[]{:S(2)}) async-start(s8[8388608]{0:T(1024)(128)(4,1)} %bitcast.406), calls=%async_computation.11 | async-start | bytes 8388608
  77.0 34.8 %copy-start.1 = (f32[2,8,8,128]{3,2,1,0:T(8,128)S(1)}, f32[2,8,8,128]{3,2,1,0:T(8,128)}, u32[]{:S(2)}) copy-start(f32[2,8,8,128]{3,2,1,0:T(8,128)} %param.5) | copy-start | bytes 196612
  124.2 125.2 %reduce-scatter.10.cloned.1.call-start = ((), (), s32[]{:S(2)}) async-start(), calls=%async_computation.7 | async-start | bytes 655360 | tf_op jit(solution)/shard_map/reduce_scatter | solution.py:72
  154.3 26.9 %slice-start.2 = ((s8[8388608]{0:T(1024)(128)(4,1)}), s8[4194304]{0:T(1024)(128)(4,1)S(1)}, s32[]{:S(2)}) async-start(s8[8388608]{0:T(1024)(128)(4,1)} %bitcast.408), calls=%async_computation.12 | async-start | bytes 8388608
  174.2 6.9 %slice-start.3 = ((s8[8388608]{0:T(1024)(128)(4,1)}), s8[4194304]{0:T(1024)(128)(4,1)S(1)}, s32[]{:S(2)}) async-start(s8[8388608]{0:T(1024)(128)(4,1)} %bitcast.408), calls=%async_computation.13 | async-start | bytes 8388608
  228.3 125.3 %reduce-scatter.12.cloned.1.call-start = ((), (), s32[]{:S(2)}) async-start(), calls=%async_computation.8 | async-start | bytes 655360 | tf_op jit(solution)/shard_map/reduce_scatter | solution.py:72
  257.9 27.3 %slice-start.4 = ((s8[8388608]{0:T(1024)(128)(4,1)}), s8[4194304]{0:T(1024)(128)(4,1)S(1)}, s32[]{:S(2)}) async-start(s8[8388608]{0:T(1024)(128)(4,1)} %bitcast.410), calls=%async_computation.14 | async-start | bytes 8388608
  278.4 6.9 %slice-start.5 = ((s8[8388608]{0:T(1024)(128)(4,1)}), s8[4194304]{0:T(1024)(128)(4,1)S(1)}, s32[]{:S(2)}) async-start(s8[8388608]{0:T(1024)(128)(4,1)} %bitcast.410), calls=%async_computation.15 | async-start | bytes 8388608
  332.6 125.0 %reduce-scatter.14.cloned.1.call-start = ((), (), s32[]{:S(2)}) async-start(), calls=%async_computation.9 | async-start | bytes 655360 | tf_op jit(solution)/shard_map/reduce_scatter | solution.py:72
  362.7 26.9 %slice-start.6 = ((s8[8388608]{0:T(1024)(128)(4,1)}), s8[4194304]{0:T(1024)(128)(4,1)S(1)}, s32[]{:S(2)}) async-start(s8[8388608]{0:T(1024)(128)(4,1)} %bitcast.412), calls=%async_computation.16 | async-start | bytes 8388608
  382.7 6.9 %slice-start.7 = ((s8[8388608]{0:T(1024)(128)(4,1)}), s8[4194304]{0:T(1024)(128)(4,1)S(1)}, s32[]{:S(2)}) async-start(s8[8388608]{0:T(1024)(128)(4,1)} %bitcast.412), calls=%async_computation.17 | async-start | bytes 8388608
  465.7 27.9 %slice-start.8 = ((s8[8388608]{0:T(1024)(128)(4,1)}), s8[4194304]{0:T(1024)(128)(4,1)S(1)}, s32[]{:S(2)}) async-start(s8[8388608]{0:T(1024)(128)(4,1)} %bitcast.414), calls=%async_computation.18 | async-start | bytes 8388608
  486.6 6.9 %slice-start.9 = ((s8[8388608]{0:T(1024)(128)(4,1)}), s8[4194304]{0:T(1024)(128)(4,1)S(1)}, s32[]{:S(2)}) async-start(s8[8388608]{0:T(1024)(128)(4,1)} %bitcast.414), calls=%async_computation.19 | async-start | bytes 8388608
Sparse Core Ops, SparseCore 0:
  16.7 24.3 reduce-scatter.5
  124.3 20.9 reduce-scatter.7
  228.4 20.8 reduce-scatter.9
  332.7 20.7 reduce-scatter.11
  436.8 20.7 reduce-scatter.13
where the time goes:
time: 545 us; the launch traced here: 536 us
  blocking collectives  268 us (49%)
  matrix products  120 us (22%)
  waiting for transfers between devices  106 us (19%)
  between operations  21 us (4%)
  other arithmetic  15 us (3%)
  local copies, waits for them, and re-layouts  5.9 us (1%)
    psum x5, blocking collectives, on_device(): lax.psum((jnp.sum(direction * direction), jnp.sum(image * image)), ('freq...  152 us
    reduce_scatter x5, waiting for transfers between devices, on_device(): lax.psum_scatter(jnp.stack([partial_real, partial_imag]).astype(jnp.bfloa...  106 us
    all_gather x5, blocking collectives, on_device(): add_segment = lax.all_gather(rounded_direction, 'recv', axis=3, tiled=True)  80.4 us
    all_gather x5, blocking collectives, on_device(): lax.all_gather(flattened.astype(jnp.bfloat16), 'freq', axis=1, tiled=True)  35.6 us
    dot_general x40, matrix products, high_dot(): return jnp.dot(left, right, precision=lax.Precision.HIGHEST)  19.8 us
    dot_general x5, matrix products, on_device(): jnp.einsum('fbs,frs->fbr', add_segment[0], imag_operator, preferred_eleme...  17.6 us
    dot_general x5, matrix products, on_device(): jnp.einsum('fbs,frs->fbr', add_segment[1], imag_operator, preferred_eleme...  16.9 us
    dot_general x5, matrix products, on_device(): jnp.einsum('fbr,frs->fbs', rounded_residual[1], imag_operator, preferred_...  14.7 us
  transfers between devices with their start and end apart: 5, of which 5 were waited for; matrix products, arithmetic and copies ran while one was open for 0% of the time, Pallas kernels for 0%

commit v1 on v0

--- a/solution.py
+++ b/solution.py
@@ -3,6 +3,7 @@
 import jax.numpy as jnp
 from jax import lax
 from jax.sharding import PartitionSpec as P
+from jax.lax import psum
 
 SBLK = 128
 ITERS = 5
@@ -104,8 +105,14 @@
             "fbs,frs->fbr", add_segment[1], real_operator, preferred_element_type=jnp.float32
         )
         image = jnp.stack([image_real, image_imag])
-        direction_power, image_energy = lax.psum(
-            (jnp.sum(direction * direction), jnp.sum(image * image)), ("freq", "recv")
+
+        def read_the_strings(patch, net_axis, along_axis="freq"):
+            for i in (net_axis, along_axis):
+                patch = psum(patch, i)
+            return patch
+
+        direction_power, image_energy = read_the_strings(
+            (jnp.sum(direction * direction), jnp.sum(image * image)), "recv"
         )
         step_length = direction_power / (image_energy + 1e-06)
         reflect = reflect + step_length * direction

time: 545 us -> 470 us (0.86)
  blocking collectives: 268 us -> 195 us
    psum x5 -> x10, blocking collectives: 152 us -> 79.4 us  [read_the_strings(): patch = psum(patch, i)]
where the time goes in v1:
time: 470 us; the launch traced here: 461 us
  blocking collectives  195 us (41%)
  matrix products  120 us (26%)
  waiting for transfers between devices  104 us (22%)
  between operations  21 us (4%)
  other arithmetic  15 us (3%)
  local copies, waits for them, and re-layouts  5.9 us (1%)
    reduce_scatter x5, waiting for transfers between devices, on_device(): lax.psum_scatter(jnp.stack([partial_real, partial_imag]).astype(jnp.bfloa...  104 us
    all_gather x5, blocking collectives, on_device(): add_segment = lax.all_gather(rounded_direction, 'recv', axis=3, tiled=True)  80.4 us
    psum x10, blocking collectives, read_the_strings(): patch = psum(patch, i)  79.4 us
    all_gather x5, blocking collectives, on_device(): lax.all_gather(flattened.astype(jnp.bfloat16), 'freq', axis=1, tiled=True)  35.3 us
    dot_general x40, matrix products, high_dot(): return jnp.dot(left, right, precision=lax.Precision.HIGHEST)  19.8 us
    dot_general x5, matrix products, on_device(): jnp.einsum('fbs,frs->fbr', add_segment[0], imag_operator, preferred_eleme...  17.6 us
    dot_general x5, matrix products, on_device(): jnp.einsum('fbs,frs->fbr', add_segment[1], imag_operator, preferred_eleme...  16.9 us
    dot_general x5, matrix products, on_device(): jnp.einsum('fbr,frs->fbs', rounded_residual[1], imag_operator, preferred_...  14.7 us
  transfers between devices with their start and end apart: 5, of which 5 were waited for; matrix products, arithmetic and copies ran while one was open for 0% of the time, Pallas kernels for 0%

profile of v1, /device:TPU:0, one launch (start us, length us, event | category | flops | bytes accessed | tf_op | source)
XLA Modules:
  0.0 460.6 jit_solution(11742091682390537614)
XLA Ops:
  8.1 3.0 fusion.46
  11.0 3.3 fusion.48
  16.9 1.8 select_reduce_fusion.1
  18.7 22.4 %reduce-scatter.6.cloned.1.call-done = bf16[2,8,8,512]{3,2,1,0:T(8,128)(2,1)} async-done(((bf16[2,8,8,2048]{3,2,1,0:T(8,128)(2,1)}), bf16[2,8,8,512]{3,2,1,0:T(8,128)(2,1)}) %reduce-scatter.6.cloned.1.call-update) | async-done | bytes 131088 | tf_op jit(solution)/shard_map/reduce_scatter | solution.py:73
  42.1 7.1 %all_gather.30 = bf16[2,32,4096]{2,1,0:T(8,128)(2,1)S(1)} all-gather(bf16[2,8,4096]{2,1,0:T(8,128)(2,1)S(1)} %convert_element_type.125), channel_id=1, replica_groups=mesh['groups'=2,'freq'=4,'recv'=4] {'freq'}, dimensions={1}, use_global_device_ids=true | all-gather | bytes 655360 | tf_op jit(solution)/shard_map/all_gather | solution.py:81
  54.0 16.1 %all_gather.31 = bf16[2,8,8,2048]{3,2,1,0:T(8,128)(2,1)S(1)} all-gather(bf16[2,8,8,512]{3,2,1,0:T(8,128)(2,1)S(1)} %get-tuple-element.37), channel_id=1, replica_groups=mesh['groups'=2,'freq'=4,'recv'=4] {'recv'}, dimensions={3}, use_global_device_ids=true | all-gather | bytes 655360 | tf_op jit(solution)/shard_map/all_gather | solution.py:96
  70.1 3.5 fusion.42
  73.6 3.4 fusion.44
  77.1 1.2 fusion.189
  78.2 1.2 fusion.183
  80.1 9.4 %all-reduce.4 = (f32[]{:T(128)}, f32[]{:T(128)}) all-reduce(f32[]{:T(128)} %get-tuple-element.36, f32[]{:T(128)} %multiply_reduce_fusion.9), channel_id=1, replica_groups=mesh['groups'=2,'freq'=4,'recv'=4] {'recv'}, use_global_device_ids=true, to_apply=%region_4.5 | all-reduce | flops 2 | bytes 16 | tf_op jit(solution)/shard_map/psum | solution.py:111
  89.5 6.4 %all-reduce.9 = (f32[]{:T(128)}, f32[]{:T(128)}) all-reduce(f32[]{:T(128)} %get-tuple-element.12, f32[]{:T(128)} %get-tuple-element.13), channel_id=1, replica_groups=mesh['groups'=2,'freq'=4,'recv'=4] {'freq'}, use_global_device_ids=true, to_apply=%region_5.6 | all-reduce | flops 2 | bytes 16 | tf_op jit(solution)/shard_map/psum | solution.py:111
  97.3 2.8 fusion.38
  100.1 2.8 fusion.40
  103.0 2.9 fusion.159
  105.8 2.9 fusion.156
  109.6 20.4 %reduce-scatter.8.cloned.1.call-done = bf16[2,8,8,512]{3,2,1,0:T(8,128)(2,1)} async-done(((bf16[2,8,8,2048]{3,2,1,0:T(8,128)(2,1)}), bf16[2,8,8,512]{3,2,1,0:T(8,128)(2,1)}) %reduce-scatter.8.cloned.1.call-update) | async-done | bytes 131088 | tf_op jit(solution)/shard_map/reduce_scatter | solution.py:73
  130.9 7.1 %all_gather.32 = bf16[2,32,4096]{2,1,0:T(8,128)(2,1)S(1)} all-gather(bf16[2,8,4096]{2,1,0:T(8,128)(2,1)S(1)} %convert_element_type.128), channel_id=1, replica_groups=mesh['groups'=2,'freq'=4,'recv'=4] {'freq'}, dimensions={1}, use_global_device_ids=true | all-gather | bytes 655360 | tf_op jit(solution)/shard_map/all_gather | solution.py:81
  142.9 16.1 %all_gather.33 = bf16[2,8,8,2048]{3,2,1,0:T(8,128)(2,1)S(1)} all-gather(bf16[2,8,8,512]{3,2,1,0:T(8,128)(2,1)S(1)} %get-tuple-element.35), channel_id=1, replica_groups=mesh['groups'=2,'freq'=4,'recv'=4] {'recv'}, dimensions={3}, use_global_device_ids=true | all-gather | bytes 655360 | tf_op jit(solution)/shard_map/all_gather | solution.py:96
  159.0 3.5 fusion.34
  162.5 3.4 fusion.36
  165.9 1.2 fusion.201
  167.1 1.2 fusion.195
  168.9 9.4 %all-reduce.3 = (f32[]{:T(128)}, f32[]{:T(128)}) all-reduce(f32[]{:T(128)} %get-tuple-element.34, f32[]{:T(128)} %multiply_reduce_fusion.8), channel_id=1, replica_groups=mesh['groups'=2,'freq'=4,'recv'=4] {'recv'}, use_global_device_ids=true, to_apply=%region_11.12 | all-reduce | flops 2 | bytes 16 | tf_op jit(solution)/shard_map/psum | solution.py:111
  178.3 6.5 %all-reduce.8 = (f32[]{:T(128)}, f32[]{:T(128)}) all-reduce(f32[]{:T(128)} %get-tuple-element.10, f32[]{:T(128)} %get-tuple-element.11), channel_id=1, replica_groups=mesh['groups'=2,'freq'=4,'recv'=4] {'freq'}, use_global_device_ids=true, to_apply=%region_12.13 | all-reduce | flops 2 | bytes 16 | tf_op jit(solution)/shard_map/psum | solution.py:111
  186.2 2.8 fusion.30
  189.0 2.8 fusion.32
  191.8 2.9 fusion.165
  194.7 2.9 fusion.162
  198.5 20.3 %reduce-scatter.10.cloned.1.call-done = bf16[2,8,8,512]{3,2,1,0:T(8,128)(2,1)} async-done(((bf16[2,8,8,2048]{3,2,1,0:T(8,128)(2,1)}), bf16[2,8,8,512]{3,2,1,0:T(8,128)(2,1)}) %reduce-scatter.10.cloned.1.call-update) | async-done | bytes 131088 | tf_op jit(solution)/shard_map/reduce_scatter | solution.py:73
  219.7 7.1 %all_gather.34 = bf16[2,32,4096]{2,1,0:T(8,128)(2,1)S(1)} all-gather(bf16[2,8,4096]{2,1,0:T(8,128)(2,1)S(1)} %convert_element_type.131), channel_id=1, replica_groups=mesh['groups'=2,'freq'=4,'recv'=4] {'freq'}, dimensions={1}, use_global_device_ids=true | all-gather | bytes 655360 | tf_op jit(solution)/shard_map/all_gather | solution.py:81
  231.7 16.1 %all_gather.35 = bf16[2,8,8,2048]{3,2,1,0:T(8,128)(2,1)S(1)} all-gather(bf16[2,8,8,512]{3,2,1,0:T(8,128)(2,1)S(1)} %get-tuple-element.33), channel_id=1, replica_groups=mesh['groups'=2,'freq'=4,'recv'=4] {'recv'}, dimensions={3}, use_global_device_ids=true | all-gather | bytes 655360 | tf_op jit(solution)/shard_map/all_gather | solution.py:96
  247.8 3.5 fusion.26
  251.3 3.4 fusion.28
  254.7 1.2 fusion.213
  255.9 1.2 fusion.207
  257.7 9.4 %all-reduce.2 = (f32[]{:T(128)}, f32[]{:T(128)}) all-reduce(f32[]{:T(128)} %get-tuple-element.32, f32[]{:T(128)} %multiply_reduce_fusion.7), channel_id=1, replica_groups=mesh['groups'=2,'freq'=4,'recv'=4] {'recv'}, use_global_device_ids=true, to_apply=%region_18.19 | all-reduce | flops 2 | bytes 16 | tf_op jit(solution)/shard_map/psum | solution.py:111
  267.2 6.7 %all-reduce.7 = (f32[]{:T(128)}, f32[]{:T(128)}) all-reduce(f32[]{:T(128)} %get-tuple-element.8, f32[]{:T(128)} %get-tuple-element.9), channel_id=1, replica_groups=mesh['groups'=2,'freq'=4,'recv'=4] {'freq'}, use_global_device_ids=true, to_apply=%region_19.20 | all-reduce | flops 2 | bytes 16 | tf_op jit(solution)/shard_map/psum | solution.py:111
  275.2 2.8 fusion.22
  278.0 2.8 fusion.24
  280.9 2.9 fusion.171
  283.7 2.9 fusion.168
  287.5 20.2 %reduce-scatter.12.cloned.1.call-done = bf16[2,8,8,512]{3,2,1,0:T(8,128)(2,1)} async-done(((bf16[2,8,8,2048]{3,2,1,0:T(8,128)(2,1)}), bf16[2,8,8,512]{3,2,1,0:T(8,128)(2,1)}) %reduce-scatter.12.cloned.1.call-update) | async-done | bytes 131088 | tf_op jit(solution)/shard_map/reduce_scatter | solution.py:73
  308.7 6.9 %all_gather.36 = bf16[2,32,4096]{2,1,0:T(8,128)(2,1)S(1)} all-gather(bf16[2,8,4096]{2,1,0:T(8,128)(2,1)S(1)} %convert_element_type.134), channel_id=1, replica_groups=mesh['groups'=2,'freq'=4,'recv'=4] {'freq'}, dimensions={1}, use_global_device_ids=true | all-gather | bytes 655360 | tf_op jit(solution)/shard_map/all_gather | solution.py:81
  320.5 16.1 %all_gather.37 = bf16[2,8,8,2048]{3,2,1,0:T(8,128)(2,1)S(1)} all-gather(bf16[2,8,8,512]{3,2,1,0:T(8,128)(2,1)S(1)} %get-tuple-element.31), channel_id=1, replica_groups=mesh['groups'=2,'freq'=4,'recv'=4] {'recv'}, dimensions={3}, use_global_device_ids=true | all-gather | bytes 655360 | tf_op jit(solution)/shard_map/all_gather | solution.py:96
  336.6 3.5 fusion.18
  340.2 3.4 fusion.20
  343.5 1.2 fusion.225
  344.7 1.2 fusion.219
  346.6 9.4 %all-reduce.1 = (f32[]{:T(128)}, f32[]{:T(128)}) all-reduce(f32[]{:T(128)} %get-tuple-element.30, f32[]{:T(128)} %multiply_reduce_fusion.6), channel_id=1, replica_groups=mesh['groups'=2,'freq'=4,'recv'=4] {'recv'}, use_global_device_ids=true, to_apply=%region_25.26 | all-reduce | flops 2 | bytes 16 | tf_op jit(solution)/shard_map/psum | solution.py:111
  356.0 6.4 %all-reduce.6 = (f32[]{:T(128)}, f32[]{:T(128)}) all-reduce(f32[]{:T(128)} %get-tuple-element.6, f32[]{:T(128)} %get-tuple-element.7), channel_id=1, replica_groups=mesh['groups'=2,'freq'=4,'recv'=4] {'freq'}, use_global_device_ids=true, to_apply=%region_26.27 | all-reduce | flops 2 | bytes 16 | tf_op jit(solution)/shard_map/psum | solution.py:111
  363.8 2.8 fusion.14
  366.6 2.8 fusion.16
  369.5 2.9 fusion.177
  372.3 2.9 fusion.174
  376.1 20.4 %reduce-scatter.14.cloned.1.call-done = bf16[2,8,8,512]{3,2,1,0:T(8,128)(2,1)} async-done(((bf16[2,8,8,2048]{3,2,1,0:T(8,128)(2,1)}), bf16[2,8,8,512]{3,2,1,0:T(8,128)(2,1)}) %reduce-scatter.14.cloned.1.call-update) | async-done | bytes 131088 | tf_op jit(solution)/shard_map/reduce_scatter | solution.py:73
  397.4 7.1 %all_gather.38 = bf16[2,32,4096]{2,1,0:T(8,128)(2,1)S(1)} all-gather(bf16[2,8,4096]{2,1,0:T(8,128)(2,1)S(1)} %convert_element_type.137), channel_id=1, replica_groups=mesh['groups'=2,'freq'=4,'recv'=4] {'freq'}, dimensions={1}, use_global_device_ids=true | all-gather | bytes 655360 | tf_op jit(solution)/shard_map/all_gather | solution.py:81
  409.4 16.1 %all_gather.39 = bf16[2,8,8,2048]{3,2,1,0:T(8,128)(2,1)S(1)} all-gather(bf16[2,8,8,512]{3,2,1,0:T(8,128)(2,1)S(1)} %get-tuple-element.28), channel_id=1, replica_groups=mesh['groups'=2,'freq'=4,'recv'=4] {'recv'}, dimensions={3}, use_global_device_ids=true | all-gather | bytes 655360 | tf_op jit(solution)/shard_map/all_gather | solution.py:96
  425.5 3.5 fusion.10
  429.0 3.4 fusion.12
  432.4 1.2 fusion.237
  433.6 1.2 fusion.231
  435.4 9.4 %all-reduce = (f32[]{:T(128)}, f32[]{:T(128)}) all-reduce(f32[]{:T(128)} %get-tuple-element.29, f32[]{:T(128)} %multiply_reduce_fusion.5), channel_id=1, replica_groups=mesh['groups'=2,'freq'=4,'recv'=4] {'recv'}, use_global_device_ids=true, to_apply=%region_32.33 | all-reduce | flops 2 | bytes 16 | tf_op jit(solution)/shard_map/psum | solution.py:111
  444.8 6.3 %all-reduce.5 = (f32[]{:T(128)}, f32[]{:T(128)}) all-reduce(f32[]{:T(128)} %get-tuple-element.4, f32[]{:T(128)} %get-tuple-element.5), channel_id=1, replica_groups=mesh['groups'=2,'freq'=4,'recv'=4] {'freq'}, use_global_device_ids=true, to_apply=%region_33.34 | all-reduce | flops 2 | bytes 16 | tf_op jit(solution)/shard_map/psum | solution.py:111
  (126 shorter events, 40.5 us)
Async XLA Ops:
  7.2 34.0 %reduce-scatter.6.cloned.1.call-start = ((), (), s32[]{:S(2)}) async-start(), calls=%async_computation.5 | async-start | bytes 655360 | tf_op jit(solution)/shard_map/reduce_scatter | solution.py:73
  8.1 6.3 %copy-start = (bf16[2,8,128,2048]{3,2,1,0:T(8,128)(2,1)S(1)}, bf16[2,8,128,2048]{3,2,1,0:T(8,128)(2,1)}, u32[]{:S(2)}) copy-start(bf16[2,8,128,2048]{3,2,1,0:T(8,128)(2,1)} %param.4) | copy-start | bytes 25165828
  15.1 1.6 copy-start.2
  15.1 1.7 copy-start.3
  16.6 113.3 %reduce-scatter.8.cloned.1.call-start = ((), (), s32[]{:S(2)}) async-start(), calls=%async_computation.6 | async-start | bytes 655360 | tf_op jit(solution)/shard_map/reduce_scatter | solution.py:73
  50.2 26.9 %slice-start = ((s8[8388608]{0:T(1024)(128)(4,1)}), s8[4194304]{0:T(1024)(128)(4,1)S(1)}, s32[]{:S(2)}) async-start(s8[8388608]{0:T(1024)(128)(4,1)} %bitcast.406), calls=%async_computation.10 | async-start | bytes 8388608
  70.1 6.9 %slice-start.1 = ((s8[8388608]{0:T(1024)(128)(4,1)}), s8[4194304]{0:T(1024)(128)(4,1)S(1)}, s32[]{:S(2)}) async-start(s8[8388608]{0:T(1024)(128)(4,1)} %bitcast.406), calls=%async_computation.11 | async-start | bytes 8388608
  77.0 20.2 %copy-start.1 = (f32[2,8,8,128]{3,2,1,0:T(8,128)S(1)}, f32[2,8,8,128]{3,2,1,0:T(8,128)}, u32[]{:S(2)}) copy-start(f32[2,8,8,128]{3,2,1,0:T(8,128)} %param.5) | copy-start | bytes 196612
  109.6 109.2 %reduce-scatter.10.cloned.1.call-start = ((), (), s32[]{:S(2)}) async-start(), calls=%async_computation.7 | async-start | bytes 655360 | tf_op jit(solution)/shard_map/reduce_scatter | solution.py:73
  139.0 26.9 %slice-start.2 = ((s8[8388608]{0:T(1024)(128)(4,1)}), s8[4194304]{0:T(1024)(128)(4,1)S(1)}, s32[]{:S(2)}) async-start(s8[8388608]{0:T(1024)(128)(4,1)} %bitcast.408), calls=%async_computation.12 | async-start | bytes 8388608
  159.0 6.9 %slice-start.3 = ((s8[8388608]{0:T(1024)(128)(4,1)}), s8[4194304]{0:T(1024)(128)(4,1)S(1)}, s32[]{:S(2)}) async-start(s8[8388608]{0:T(1024)(128)(4,1)} %bitcast.408), calls=%async_computation.13 | async-start | bytes 8388608
  198.4 109.3 %reduce-scatter.12.cloned.1.call-start = ((), (), s32[]{:S(2)}) async-start(), calls=%async_computation.8 | async-start | bytes 655360 | tf_op jit(solution)/shard_map/reduce_scatter | solution.py:73
  227.3 27.4 %slice-start.4 = ((s8[8388608]{0:T(1024)(128)(4,1)}), s8[4194304]{0:T(1024)(128)(4,1)S(1)}, s32[]{:S(2)}) async-start(s8[8388608]{0:T(1024)(128)(4,1)} %bitcast.410), calls=%async_computation.14 | async-start | bytes 8388608
  247.8 6.9 %slice-start.5 = ((s8[8388608]{0:T(1024)(128)(4,1)}), s8[4194304]{0:T(1024)(128)(4,1)S(1)}, s32[]{:S(2)}) async-start(s8[8388608]{0:T(1024)(128)(4,1)} %bitcast.410), calls=%async_computation.15 | async-start | bytes 8388608
  287.5 109.0 %reduce-scatter.14.cloned.1.call-start = ((), (), s32[]{:S(2)}) async-start(), calls=%async_computation.9 | async-start | bytes 655360 | tf_op jit(solution)/shard_map/reduce_scatter | solution.py:73
  316.7 26.9 %slice-start.6 = ((s8[8388608]{0:T(1024)(128)(4,1)}), s8[4194304]{0:T(1024)(128)(4,1)S(1)}, s32[]{:S(2)}) async-start(s8[8388608]{0:T(1024)(128)(4,1)} %bitcast.412), calls=%async_computation.16 | async-start | bytes 8388608
  336.6 6.9 %slice-start.7 = ((s8[8388608]{0:T(1024)(128)(4,1)}), s8[4194304]{0:T(1024)(128)(4,1)S(1)}, s32[]{:S(2)}) async-start(s8[8388608]{0:T(1024)(128)(4,1)} %bitcast.412), calls=%async_computation.17 | async-start | bytes 8388608
  404.5 27.9 %slice-start.8 = ((s8[8388608]{0:T(1024)(128)(4,1)}), s8[4194304]{0:T(1024)(128)(4,1)S(1)}, s32[]{:S(2)}) async-start(s8[8388608]{0:T(1024)(128)(4,1)} %bitcast.414), calls=%async_computation.18 | async-start | bytes 8388608
  425.5 6.9 %slice-start.9 = ((s8[8388608]{0:T(1024)(128)(4,1)}), s8[4194304]{0:T(1024)(128)(4,1)S(1)}, s32[]{:S(2)}) async-start(s8[8388608]{0:T(1024)(128)(4,1)} %bitcast.414), calls=%async_computation.19 | async-start | bytes 8388608
Sparse Core Ops, SparseCore 0:
  16.7 24.3 reduce-scatter.5
  109.7 20.2 reduce-scatter.7
  198.6 20.1 reduce-scatter.9
  287.6 20.1 reduce-scatter.11
  376.2 20.2 reduce-scatter.13
